TPU v7x, 256 devices: a whole 4x4x8 slice. The times are simulated.
256 devices in a mesh: dp: 16 (over x, y_hi, core), mp: 16 (over y_lo, z).
Axes of the slice: x: 4, y: 4 (y_hi: 2, y_lo: 2; y = y_hi * 2 + y_lo), z: 8, core: 2. Of those that a mesh axis runs over, the one named last changes fastest.
Arguments:
- tokens: bfloat16 [4096, 4096], P('dp'), may hold values from -32 to 32
- weights: bfloat16 [4096, 2, 3, 4096], P('dp', None, None, 'mp'), may hold values from -1 to 1
- block_modality: int32 [32], replicated, may hold values from 0 to 1
- doc_ids: int32 [4096], replicated, may hold values from 0 to 31, never falling along the last dimension, each value on 1 to 1024 neighbouring positions
- grad_out: bfloat16 [4096, 4096], P('dp', 'mp'), may hold values from -6 to 6
Outputs:
- attended: bfloat16 [4096, 4096], P('dp', 'mp')
- grad_tokens: bfloat16 [4096, 4096], P('dp', 'mp')
- grad_weights: bfloat16 [4096, 2, 3, 4096], P('dp', None, None, 'mp')
Inputs may be any that keep to these rules, and one draw needn't show every extreme that they name: doc_ids never falls along the sequence; a document is a run of equal ids of at most 1024 tokens, and one document has exactly 1024.
All inputs are finite; a program needn't handle non-finite values.
Results may differ from a plain program's by a relative error of at most 0.025.
Values may be sent and summed in bfloat16 or wider, within the bound.
No kernel may reach another device: no remote copies, remote signals or barrier semaphores. Data moves between devices by JAX's collectives and lax.ppermute only.
A program may use at most 128 MiB of HBM per device.

v0:
```python
import jax
import jax.numpy as jnp
from jax import lax
from jax.sharding import PartitionSpec as P

HD = 128
BLOCK = 128
SPAN = 4


def shifted(block, axis, distance):
    devices = range(lax.axis_size(axis))
    route = [(i - distance, i) for i in devices if i - distance in devices]
    return lax.ppermute(block, axis, route)


def split_by_modality(rows, is_image):
    zeros = jnp.zeros_like(rows)
    text = jnp.where(is_image[:, None], zeros, rows)
    image = jnp.where(is_image[:, None], rows, zeros)
    return jnp.stack([text, image], axis=2).reshape(rows.shape[0], 2 * rows.shape[1])


def split_by_modality_major(rows, is_image):
    zeros = jnp.zeros_like(rows)
    text = jnp.where(is_image[:, None], zeros, rows)
    image = jnp.where(is_image[:, None], rows, zeros)
    return jnp.concatenate([text, image], axis=1)


def dp_ring(size):
    if size % 4:
        return list(range(size))
    chips = size // 2
    order = [2 * x for x in range(chips // 2)] + [2 * x + 1 for x in reversed(range(chips // 2))]
    return [2 * chip + core for chip in order for core in range(2)]


def ring_blocks(rows, ring, axis):
    shape = rows.shape
    blocks = rows.reshape(shape[:axis] + (len(ring), shape[axis] // len(ring)) + shape[axis + 1 :])
    return jnp.take(blocks, jnp.array(ring, jnp.int32), axis=axis).reshape(shape)


def on_device(tokens, weights, block_modality, doc_ids, grad_out):
    local_rows = tokens.shape[0]
    width_rows = weights.shape[0]
    head_width = weights.shape[3]
    head_count = head_width // HD
    dp_devices = lax.axis_size("dp")
    mp_devices = lax.axis_size("mp")
    local_blocks = local_rows // BLOCK
    front_pad = SPAN * local_rows
    window_len = front_pad + local_rows
    my_index = lax.axis_index("dp")
    scale_factor = HD ** (-0.5)
    token_image = jnp.repeat(block_modality, BLOCK) == 1
    my_image = lax.dynamic_slice_in_dim(token_image, my_index * local_rows, local_rows, 0)
    ring = dp_ring(dp_devices)
    inverse = [ring.index(k) for k in range(dp_devices)]
    flat_weights = (
        weights.reshape(width_rows, 2, 3 * head_width)
        .transpose(1, 0, 2)
        .reshape(2 * width_rows, 3 * head_width)
    )
    stacked_weights = lax.all_gather(
        flat_weights, "dp", axis=0, tiled=True, axis_index_groups=[ring]
    )
    columns = lax.all_to_all(tokens, "dp", split_axis=1, concat_axis=0, tiled=True)
    ring_columns = split_by_modality_major(
        ring_blocks(columns, ring, 0), ring_blocks(token_image, ring, 0)
    )
    ring_tokens = ring_blocks(tokens, ring, 1).reshape(local_rows, dp_devices, 1, width_rows)
    ring_tokens = jnp.concatenate(
        [
            jnp.where(my_image[:, None, None, None], jnp.zeros_like(ring_tokens), ring_tokens),
            jnp.where(my_image[:, None, None, None], ring_tokens, jnp.zeros_like(ring_tokens)),
        ],
        axis=2,
    ).reshape(local_rows, -1)
    stacked_weights, ring_columns, ring_tokens = lax.optimization_barrier(
        (stacked_weights, ring_columns, ring_tokens)
    )
    block_weights = stacked_weights.reshape(dp_devices, 2, width_rows, 3 * head_width)
    key_values = (
        jnp.dot(ring_tokens, stacked_weights[:, head_width:], preferred_element_type=jnp.float32)
        .astype(jnp.bfloat16)
        .reshape(local_rows, 2, head_count, HD)
    )
    received = []
    for distance in range(SPAN, 0, -1):
        received.append(shifted(key_values, "dp", distance))
    queries = (
        jnp.dot(ring_tokens, stacked_weights[:, :head_width], preferred_element_type=jnp.float32)
        .astype(jnp.bfloat16)
        .reshape(local_rows, head_count, HD)
    )
    window = jnp.concatenate(received + [key_values], 0)
    key_rows = window[:, 0]
    value_rows = window[:, 1]
    docs_pad = jnp.concatenate([jnp.full((front_pad,), -1, jnp.int32), doc_ids], 0)
    key_docs = lax.dynamic_slice_in_dim(docs_pad, my_index * local_rows, window_len, 0)
    query_docs = lax.dynamic_slice_in_dim(doc_ids, my_index * local_rows, local_rows, 0)
    offsets = jnp.arange(window_len, dtype=jnp.int32) - front_pad
    allowed = (key_docs[None, :] == query_docs[:, None]) & (
        offsets[None, :] <= jnp.arange(local_rows, dtype=jnp.int32)[:, None]
    )
    scores = (
        jnp.einsum("qhd,khd->hqk", queries, key_rows, preferred_element_type=jnp.float32)
        * scale_factor
    )
    scores = jnp.where(allowed[None], scores, -1e30)
    top_score = jnp.max(scores, axis=-1, keepdims=True)
    expos = jnp.where(allowed[None], jnp.exp(scores - top_score), 0.0)
    probs_f = expos / jnp.sum(expos, axis=-1, keepdims=True)
    probs = probs_f.astype(jnp.bfloat16)
    attended = jnp.einsum("hqk,khd->qhd", probs, value_rows, preferred_element_type=jnp.float32)
    attended = attended.astype(jnp.bfloat16).reshape(local_rows, head_width)
    upstream = grad_out.reshape(local_rows, head_count, HD)
    dprob = jnp.einsum("qhd,khd->hqk", upstream, value_rows, preferred_element_type=jnp.float32)
    row_delta = jnp.sum(probs_f * dprob, axis=-1, keepdims=True)
    dscore = (probs_f * (dprob - row_delta)).astype(jnp.bfloat16)
    grad_q = (
        jnp.einsum("hqk,khd->qhd", dscore, key_rows, preferred_element_type=jnp.float32)
        * scale_factor
    )
    grad_k = (
        jnp.einsum("hqk,qhd->khd", dscore, queries, preferred_element_type=jnp.float32)
        * scale_factor
    )
    grad_v = jnp.einsum("hqk,qhd->khd", probs, upstream, preferred_element_type=jnp.float32)
    window_grads = jnp.stack([grad_k, grad_v], 1)
    own_grads = window_grads[front_pad:]
    for distance in range(1, SPAN + 1):
        lower_edge = front_pad - distance * local_rows
        sent_block = window_grads[lower_edge : lower_edge + local_rows]
        own_grads = own_grads + shifted(sent_block.astype(jnp.bfloat16), "dp", -distance).astype(
            sent_block.dtype
        )
    dqkv = (
        jnp.concatenate([grad_q[:, None], own_grads], 1)
        .astype(jnp.bfloat16)
        .reshape(local_rows, 3 * head_width)
    )
    zeros = jnp.zeros_like(dqkv)
    parts = lax.dot_general(
        jnp.where(my_image[:, None], zeros, dqkv),
        block_weights[:, 0],
        (((1,), (2,)), ((), ())),
        preferred_element_type=jnp.float32,
    ) + lax.dot_general(
        jnp.where(my_image[:, None], dqkv, zeros),
        block_weights[:, 1],
        (((1,), (2,)), ((), ())),
        preferred_element_type=jnp.float32,
    )
    parts = jnp.take(
        parts.astype(jnp.bfloat16).transpose(1, 0, 2), jnp.array(inverse, jnp.int32), axis=0
    ).reshape(mp_devices, local_rows, -1)
    group_parts = lax.all_to_all(parts, "mp", split_axis=0, concat_axis=0, tiled=True)
    grad_tokens = jnp.sum(group_parts.astype(jnp.float32), axis=0).astype(jnp.bfloat16)
    gathered = lax.all_gather(dqkv[None], "dp", axis=0, tiled=True, axis_index_groups=[ring])
    weight_sum = lax.dot_general(
        ring_columns.reshape(dp_devices, local_rows, -1),
        gathered,
        (((0, 1), (0, 1)), ((), ())),
        preferred_element_type=jnp.float32,
    )
    grad_weights = (
        weight_sum.astype(jnp.bfloat16)
        .reshape(2, width_rows, 3 * head_width)
        .transpose(1, 0, 2)
        .reshape(width_rows, 2, 3, head_width)
    )
    return (attended, grad_tokens, grad_weights)


def solution(mesh):
    return jax.shard_map(
        on_device,
        mesh=mesh,
        in_specs=(P("dp", None), P("dp", None, None, "mp"), P(), P(), P("dp", "mp")),
        out_specs=(P("dp", "mp"), P("dp", "mp"), P("dp", None, None, "mp")),
        check_vma=False,
    )
```

profile of v0, /device:TPU:97, one launch (start us, length us, event | category | flops | bytes accessed | tf_op | source)
XLA Modules:
  0.0 262.4 jit_solution(9539630087630359603)
XLA Ops:
  10.6 3.3 %copy.77 = bf16[256,4096]{0,1:T(8,128)(2,1)S(1)} copy(bf16[256,4096]{1,0:T(8,128)(2,1)} %param.11) | data formatting | bytes 4194304 | tf_op args[0]
  13.9 2.5 copy.78
  16.4 7.7 %all-to-all-start = ((bf16[256,16,256]{2,0,1:T(8,128)(2,1)}), bf16[256,16,256]{2,0,1:T(8,128)(2,1)}, u32[]{:S(2)}, u32[]{:S(2)}) async-start(bf16[256,16,256]{2,0,1:T(8,128)(2,1)} %copy.78), calls=%async_computation | async-start | bytes 4194304 | tf_op jit(solution)/shard_map/all_to_all | solution.py:69
  24.4 2.5 gather_fusion.1
  28.1 2.3 pad_maximum_fusion.1
  30.4 6.4 %copy.80 = bf16[256,16,2,256]{0,3,2,1:T(8,128)(2,1)} copy(bf16[256,16,2,256]{3,0,1,2:T(8,128)(2,1)} %pad_maximum_fusion.1) | data formatting | bytes 8388608 | tf_op jit(solution)/shard_map/concatenate | solution.py:74
  37.3 30.9 %all-to-all-done = bf16[256,16,256]{2,0,1:T(8,128)(2,1)} async-done(((bf16[256,16,256]{2,0,1:T(8,128)(2,1)}), bf16[256,16,256]{2,0,1:T(8,128)(2,1)}, u32[]{:S(2)}, u32[]{:S(2)}) %all-to-all-start) | async-done | bytes 2097184 | tf_op jit(solution)/shard_map/all_to_all | solution.py:69
  72.7 2.4 pad_maximum_fusion
  75.0 36.4 %all-gather.3.cloned.1.call-done = bf16[8192,768]{1,0:T(8,128)(2,1)} async-done(((bf16[512,768]{1,0:T(8,128)(2,1)}), bf16[8192,768]{1,0:T(8,128)(2,1)}) %all-gather.3.cloned.1.call-update) | async-done | bytes 12582928 | tf_op jit(solution)/shard_map/all_gather | solution.py:66
  111.5 7.0 %fusion.15 = bf16[256,512]{1,0:T(8,128)(2,1)S(1)} fusion(bf16[256,8192]{0,1:T(8,128)(2,1)} %bitcast.99, bf16[8192,768]{1,0:T(8,128)(2,1)} %all-gather.3.cloned.1.call-done), kind=kOutput, calls=%fused_computation.40 | convolution fusion | flops 2147614720 | bytes 12845056 | tf_op jit(solution)/shard_map/dot_general | solution.py:86
  120.1 3.2 %collective-permute-start.1 = (bf16[256,2,2,128]{3,0,2,1:T(8,128)(2,1)S(1)}, bf16[256,2,2,128]{3,0,2,1:T(8,128)(2,1)S(1)}, u32[]{:S(2)}, u32[]{:S(2)}) collective-permute-start(bf16[256,2,2,128]{3,0,2,1:T(8,128)(2,1)S(1)} %copy.81), channel_id=1, source_target_pairs={{0,48},{16,64},{32,80},{48,96},{64,112},{80,128},{96,144},{112,160... | collective-permute-start | bytes 786440 | tf_op jit(solution)/shard_map/ppermute | solution.py:14
  123.3 4.8 %collective-permute-start.2 = (bf16[256,2,2,128]{3,0,2,1:T(8,128)(2,1)S(1)}, bf16[256,2,2,128]{3,0,2,1:T(8,128)(2,1)S(1)}, u32[]{:S(2)}, u32[]{:S(2)}) collective-permute-start(bf16[256,2,2,128]{3,0,2,1:T(8,128)(2,1)S(1)} %copy.81), channel_id=1, source_target_pairs={{0,32},{16,48},{32,64},{48,80},{64,96},{80,112},{96,128},{112,144}... | collective-permute-start | bytes 786440 | tf_op jit(solution)/shard_map/ppermute | solution.py:14
  128.1 4.7 %collective-permute-start.3 = (bf16[256,2,2,128]{3,0,2,1:T(8,128)(2,1)S(1)}, bf16[256,2,2,128]{3,0,2,1:T(8,128)(2,1)S(1)}, u32[]{:S(2)}, u32[]{:S(2)}) collective-permute-start(bf16[256,2,2,128]{3,0,2,1:T(8,128)(2,1)S(1)} %copy.81), channel_id=1, source_target_pairs={{0,16},{16,32},{32,48},{48,64},{64,80},{80,96},{96,112},{112,128},... | collective-permute-start | bytes 786440 | tf_op jit(solution)/shard_map/ppermute | solution.py:14
  132.8 5.2 %fusion.19 = bf16[256,256]{0,1:T(8,128)(2,1)S(1)} fusion(bf16[256,8192]{0,1:T(8,128)(2,1)} %bitcast.100, bf16[8192,768]{1,0:T(8,128)(2,1)} %all-gather.3.cloned.1.call-done), kind=kOutput, calls=%fused_computation.43 | convolution fusion | flops 1073807360 | bytes 8519680 | tf_op jit(solution)/shard_map/dot_general | solution.py:94
  139.3 2.6 fusion.33
  152.4 2.7 %collective-permute-done.7 = bf16[256,2,2,128]{0,3,2,1:T(8,128)(2,1)S(1)} collective-permute-done((bf16[256,2,2,128]{0,3,2,1:T(8,128)(2,1)S(1)}, bf16[256,2,2,128]{0,3,2,1:T(8,128)(2,1)S(1)}, u32[]{:S(2)}, u32[]{:S(2)}) %collective-permute-start.7) | collective-permute-done | bytes 262176 | tf_op jit(solution)/shard_map/ppermute | solution.py:14
  155.1 10.9 %collective-permute-done.6 = bf16[256,2,2,128]{0,3,2,1:T(8,128)(2,1)S(1)} collective-permute-done((bf16[256,2,2,128]{0,3,2,1:T(8,128)(2,1)S(1)}, bf16[256,2,2,128]{0,3,2,1:T(8,128)(2,1)S(1)}, u32[]{:S(2)}, u32[]{:S(2)}) %collective-permute-start.6) | collective-permute-done | bytes 262176 | tf_op jit(solution)/shard_map/ppermute | solution.py:14
  167.3 4.6 %fusion.3 = f32[256,16,256]{2,0,1:T(8,128)S(1)} fusion(bf16[256,768,1]{0,1,2:T(8,128)(2,1)S(1)} %bitcast.109, bf16[16,2,256,768]{3,2,1,0:T(8,128)(2,1)} %bitcast.102), kind=kOutput, calls=%fused_computation.8 | convolution fusion | flops 1610612736 | bytes 10878976 | tf_op jit(solution)/shard_map/dot_general | solution.py:151
  172.0 4.6 %fusion.13 = bf16[16,256,256]{2,1,0:T(8,128)(2,1)S(1)} fusion(f32[256,16,256]{2,0,1:T(8,128)S(1)} %fusion.3, bf16[256,768,1]{0,1,2:T(8,128)(2,1)S(1)} %bitcast.107, bf16[16,2,256,768]{3,2,1,0:T(8,128)(2,1)} %bitcast.103), kind=kOutput, calls=%fused_computation.31 | convolution fusion | flops 1612709888 | bytes 12976128 | tf_op jit(solution)/shard_map/dot_general | solution.py:146
  178.7 6.9 %all-to-all-start.1 = ((bf16[16,256,256]{2,1,0:T(8,128)(2,1)}), bf16[16,256,256]{2,1,0:T(8,128)(2,1)S(1)}, u32[]{:S(2)}, u32[]{:S(2)}) async-start(bf16[16,256,256]{2,1,0:T(8,128)(2,1)} %gather_fusion.3), calls=%async_computation.1 | async-start | bytes 4194304 | tf_op jit(solution)/shard_map/all_to_all | solution.py:160
  185.6 2.6 convolution_convert_fusion
  188.9 42.2 %all-to-all-done.1 = bf16[16,256,256]{2,1,0:T(8,128)(2,1)S(1)} async-done(((bf16[16,256,256]{2,1,0:T(8,128)(2,1)}), bf16[16,256,256]{2,1,0:T(8,128)(2,1)S(1)}, u32[]{:S(2)}, u32[]{:S(2)}) %all-to-all-start.1) | async-done | bytes 2097184 | tf_op jit(solution)/shard_map/all_to_all | solution.py:160
  232.1 13.8 %all-gather.5.cloned.1.call-done = bf16[16,256,768]{2,1,0:T(8,128)(2,1)} async-done(((bf16[1,256,768]{2,1,0:T(8,128)(2,1)}), bf16[16,256,768]{2,1,0:T(8,128)(2,1)}) %all-gather.5.cloned.1.call-update) | async-done | bytes 6291472 | tf_op jit(solution)/shard_map/all_gather | solution.py:162
  245.9 7.5 %bitcast_convert_fusion = bf16[512,768]{1,0:T(8,128)(2,1)S(1)} fusion(bf16[16,256,512]{2,1,0:T(8,128)(2,1)} %bitcast.98, bf16[16,256,768]{2,1,0:T(8,128)(2,1)} %all-gather.5.cloned.1.call-done), kind=kOutput, calls=%fused_computation.36 | convolution fusion | flops 3221618688 | bytes 11272192 | tf_op jit(solution)/shard_map/dot_general | solution.py:163
  (75 shorter events, 30.0 us)
Async XLA Ops:
  7.2 104.3 %all-gather.3.cloned.1.call-start = ((), (), s32[]{:S(2)}) async-start(), calls=%async_computation.2 | async-start | bytes 13369344 | tf_op jit(solution)/shard_map/all_gather | solution.py:66
  16.4 7.8 %copy-start.8 = (s32[32]{0:T(128)S(1)}, s32[32]{0:T(128)}, u32[]{:S(2)}) copy-start(s32[32]{0:T(128)} %param.13) | copy-start | bytes 388
  16.4 8.0 %copy-start.7 = (s32[16]{0:T(128)S(1)}, s32[16]{0:T(128)}, u32[]{:S(2)}) copy-start(s32[16]{0:T(128)} %constant.77.clone) | copy-start | bytes 196
  16.4 51.9 %all-to-all-start = ((bf16[256,16,256]{2,0,1:T(8,128)(2,1)}), bf16[256,16,256]{2,0,1:T(8,128)(2,1)}, u32[]{:S(2)}, u32[]{:S(2)}) async-start(bf16[256,16,256]{2,0,1:T(8,128)(2,1)} %copy.78), calls=%async_computation | async-start | bytes 4194304 | tf_op jit(solution)/shard_map/all_to_all | solution.py:69
  24.1 221.8 %all-gather.5.cloned.1.call-start = ((), (), s32[]{:S(2)}) async-start(), calls=%async_computation.3 | async-start | bytes 6684672 | tf_op jit(solution)/shard_map/all_gather | solution.py:162
  30.3 6.4 %copy-start.5 = (s32[4096]{0:T(1024)S(1)}, s32[4096]{0:T(1024)}, u32[]{:S(2)}) copy-start(s32[4096]{0:T(1024)} %param.14) | copy-start | bytes 49156
  30.4 6.5 %copy-start.4 = (bf16[256,256]{1,0:T(8,128)(2,1)S(1)}, bf16[256,256]{1,0:T(8,128)(2,1)}, u32[]{:S(2)}) copy-start(bf16[256,256]{1,0:T(8,128)(2,1)} %param.15) | copy-start | bytes 393220
  118.6 19.4 %collective-permute-start = (bf16[256,2,2,128]{3,0,2,1:T(8,128)(2,1)S(1)}, bf16[256,2,2,128]{3,0,2,1:T(8,128)(2,1)S(1)}, u32[]{:S(2)}, u32[]{:S(2)}) collective-permute-start(bf16[256,2,2,128]{3,0,2,1:T(8,128)(2,1)S(1)} %copy.81), channel_id=1, source_target_pairs={{0,64},{16,80},{32,96},{48,112},{64,128},{80,144},{96,160},{112,17... | collective-permute-start | bytes 786440 | tf_op jit(solution)/shard_map/ppermute | solution.py:14
  120.1 18.0 %collective-permute-start.1 = (bf16[256,2,2,128]{3,0,2,1:T(8,128)(2,1)S(1)}, bf16[256,2,2,128]{3,0,2,1:T(8,128)(2,1)S(1)}, u32[]{:S(2)}, u32[]{:S(2)}) collective-permute-start(bf16[256,2,2,128]{3,0,2,1:T(8,128)(2,1)S(1)} %copy.81), channel_id=1, source_target_pairs={{0,48},{16,64},{32,80},{48,96},{64,112},{80,128},{96,144},{112,160... | collective-permute-start | bytes 786440 | tf_op jit(solution)/shard_map/ppermute | solution.py:14
  123.3 14.8 %collective-permute-start.2 = (bf16[256,2,2,128]{3,0,2,1:T(8,128)(2,1)S(1)}, bf16[256,2,2,128]{3,0,2,1:T(8,128)(2,1)S(1)}, u32[]{:S(2)}, u32[]{:S(2)}) collective-permute-start(bf16[256,2,2,128]{3,0,2,1:T(8,128)(2,1)S(1)} %copy.81), channel_id=1, source_target_pairs={{0,32},{16,48},{32,64},{48,80},{64,96},{80,112},{96,128},{112,144}... | collective-permute-start | bytes 786440 | tf_op jit(solution)/shard_map/ppermute | solution.py:14
  128.1 10.1 %collective-permute-start.3 = (bf16[256,2,2,128]{3,0,2,1:T(8,128)(2,1)S(1)}, bf16[256,2,2,128]{3,0,2,1:T(8,128)(2,1)S(1)}, u32[]{:S(2)}, u32[]{:S(2)}) collective-permute-start(bf16[256,2,2,128]{3,0,2,1:T(8,128)(2,1)S(1)} %copy.81), channel_id=1, source_target_pairs={{0,16},{16,32},{32,48},{48,64},{64,80},{80,96},{96,112},{112,128},... | collective-permute-start | bytes 786440 | tf_op jit(solution)/shard_map/ppermute | solution.py:14
  138.3 1.0 copy-start.1
  141.9 2.6 %copy-start = (f32[2,256,1280]{2,1,0:T(8,128)}, f32[2,256,1280]{2,1,0:T(8,128)S(1)}, u32[]{:S(2)}) copy-start(f32[2,256,1280]{2,1,0:T(8,128)S(1)} %get-tuple-element.33) | copy-start | bytes 7864324
  145.3 6.5 %copy-start.2 = (bf16[1280,2,2,128]{3,0,2,1:T(8,128)(2,1)S(1)}, bf16[1280,2,2,128]{3,0,2,1:T(8,128)(2,1)}, u32[]{:S(2)}) copy-start(bf16[1280,2,2,128]{3,0,2,1:T(8,128)(2,1)} %copy-done.1) | copy-start | bytes 3932164
  145.6 9.5 %collective-permute-start.7 = (bf16[256,2,2,128]{0,3,2,1:T(8,128)(2,1)S(1)}, bf16[256,2,2,128]{0,3,2,1:T(8,128)(2,1)S(1)}, u32[]{:S(2)}, u32[]{:S(2)}) collective-permute-start(bf16[256,2,2,128]{0,3,2,1:T(8,128)(2,1)S(1)} %get-tuple-element.29), channel_id=1, source_target_pairs={{64,0},{80,16},{96,32},{112,48},{128,64},{144,80},{160,96},{176,11... | collective-permute-start | bytes 786440 | tf_op jit(solution)/shard_map/ppermute | solution.py:14
  147.1 19.0 %collective-permute-start.6 = (bf16[256,2,2,128]{0,3,2,1:T(8,128)(2,1)S(1)}, bf16[256,2,2,128]{0,3,2,1:T(8,128)(2,1)S(1)}, u32[]{:S(2)}, u32[]{:S(2)}) collective-permute-start(bf16[256,2,2,128]{0,3,2,1:T(8,128)(2,1)S(1)} %get-tuple-element.30), channel_id=1, source_target_pairs={{48,0},{64,16},{80,32},{96,48},{112,64},{128,80},{144,96},{160,112... | collective-permute-start | bytes 786440 | tf_op jit(solution)/shard_map/ppermute | solution.py:14
  148.4 17.7 %collective-permute-start.5 = (bf16[256,2,2,128]{0,3,2,1:T(8,128)(2,1)S(1)}, bf16[256,2,2,128]{0,3,2,1:T(8,128)(2,1)S(1)}, u32[]{:S(2)}, u32[]{:S(2)}) collective-permute-start(bf16[256,2,2,128]{0,3,2,1:T(8,128)(2,1)S(1)} %get-tuple-element.31), channel_id=1, source_target_pairs={{32,0},{48,16},{64,32},{80,48},{96,64},{112,80},{128,96},{144,112}... | collective-permute-start | bytes 786440 | tf_op jit(solution)/shard_map/ppermute | solution.py:14
  149.7 16.4 %collective-permute-start.4 = (bf16[256,2,2,128]{0,3,2,1:T(8,128)(2,1)S(1)}, bf16[256,2,2,128]{0,3,2,1:T(8,128)(2,1)S(1)}, u32[]{:S(2)}, u32[]{:S(2)}) collective-permute-start(bf16[256,2,2,128]{0,3,2,1:T(8,128)(2,1)S(1)} %get-tuple-element.28), channel_id=1, source_target_pairs={{16,0},{32,16},{48,32},{64,48},{80,64},{96,80},{112,96},{128,112},... | collective-permute-start | bytes 786440 | tf_op jit(solution)/shard_map/ppermute | solution.py:14
  166.3 1.0 copy-start.6
  178.7 6.9 %copy-start.3 = (bf16[1280,2,2,128]{3,0,2,1:T(8,128)(2,1)S(1)}, bf16[1280,2,2,128]{3,0,2,1:T(8,128)(2,1)}, u32[]{:S(2)}) copy-start(bf16[1280,2,2,128]{3,0,2,1:T(8,128)(2,1)} %copy-done.1) | copy-start | bytes 3932164
  178.7 52.5 %all-to-all-start.1 = ((bf16[16,256,256]{2,1,0:T(8,128)(2,1)}), bf16[16,256,256]{2,1,0:T(8,128)(2,1)S(1)}, u32[]{:S(2)}, u32[]{:S(2)}) async-start(bf16[16,256,256]{2,1,0:T(8,128)(2,1)} %gather_fusion.3), calls=%async_computation.1 | async-start | bytes 4194304 | tf_op jit(solution)/shard_map/all_to_all | solution.py:160
Sparse Core Ops, SparseCore 0:
  10.8 100.6 all-gather.2
  167.4 78.4 all-gather.4
where the time goes:
time: 263 us; the launch traced here: 262 us
  waiting for transfers between devices  137 us (52%)
  matrix products  37.7 us (14%)
  starting transfers between devices  35 us (13%)
  local copies, waits for them, and re-layouts  28.7 us (11%)
  between operations  14.5 us (6%)
  other arithmetic  9.41 us (4%)
    all_to_all x1, waiting for transfers between devices, on_device(): lax.all_to_all(parts, 'mp', split_axis=0, concat_axis=0, tiled=True)  42.2 us
    all_gather x1, waiting for transfers between devices, on_device(): lax.all_gather(flat_weights, 'dp', axis=0, tiled=True, axis_index_groups=...  36.4 us
    all_to_all x1, waiting for transfers between devices, on_device(): lax.all_to_all(tokens, 'dp', split_axis=1, concat_axis=0, tiled=True)  30.9 us
    ppermute x8, starting transfers between devices, shifted(): return lax.ppermute(block, axis, route)  20.3 us
    all_gather x1, waiting for transfers between devices, on_device(): lax.all_gather(dqkv[None], 'dp', axis=0, tiled=True, axis_index_groups=[r...  13.8 us
    ppermute x8, waiting for transfers between devices, shifted(): return lax.ppermute(block, axis, route)  13.7 us
    unnamed x27, local copies, waits for them, and re-layouts  9.27 us
    all_to_all x1, starting transfers between devices, on_device(): lax.all_to_all(tokens, 'dp', split_axis=1, concat_axis=0, tiled=True)  7.75 us
  transfers between devices with their start and end apart: 12, of which 6 were waited for; matrix products, arithmetic and copies ran while one was open for 18% of the time, Pallas kernels for 0%

commit v1 on v0

--- a/solution.py
+++ b/solution.py
@@ -66,7 +66,12 @@
     stacked_weights = lax.all_gather(
         flat_weights, "dp", axis=0, tiled=True, axis_index_groups=[ring]
     )
-    columns = lax.all_to_all(tokens, "dp", split_axis=1, concat_axis=0, tiled=True)
+    columns = jnp.concatenate(
+        lax.all_to_all(
+            jnp.stack(jnp.split(tokens, lax.axis_size("dp"), axis=1), axis=0), "dp", 0, 0
+        ),
+        axis=0,
+    )
     ring_columns = split_by_modality_major(
         ring_blocks(columns, ring, 0), ring_blocks(token_image, ring, 0)
     )

time: 263 us -> 263 us (level)
  local copies, waits for them, and re-layouts: 28.7 us -> 40.1 us
  waiting for transfers between devices: 137 us -> 126 us
    unnamed x27 -> x44, local copies, waits for them, and re-layouts: 9.27 us -> 18.7 us
    all_to_all x1, waiting for transfers between devices: 30.9 us -> 24.9 us  [on_device(): lax.all_to_all(jnp.stack(jnp.split(tokens, lax.axis_size('dp'), axis=1),...]
    all_gather x1, waiting for transfers between devices: 36.4 us -> 31.3 us  [on_device(): lax.all_gather(flat_weights, 'dp', axis=0, tiled=True, axis_index_groups=...]
    reshape x0 -> x1, local copies, waits for them, and re-layouts: none -> 3.99 us  [ring_blocks(): rows.reshape(shape[:axis] + (len(ring), shape[axis] // len(ring)) + shape...]
  transfers between devices with their start and end apart: 12 -> 12, of which waited for: 6 -> 6; matrix products, arithmetic and copies ran while one was open for 18% -> 22% of each run, Pallas kernels for 0% -> 0%
where the time goes in v1:
time: 263 us; the launch traced here: 262 us
  waiting for transfers between devices  126 us (48%)
  local copies, waits for them, and re-layouts  40.1 us (15%)
  matrix products  37.7 us (14%)
  starting transfers between devices  34.9 us (13%)
  between operations  14.5 us (6%)
  other arithmetic  9.41 us (4%)
    all_to_all x1, waiting for transfers between devices, on_device(): lax.all_to_all(parts, 'mp', split_axis=0, concat_axis=0, tiled=True)  42.2 us
    all_gather x1, waiting for transfers between devices, on_device(): lax.all_gather(flat_weights, 'dp', axis=0, tiled=True, axis_index_groups=...  31.3 us
    all_to_all x1, waiting for transfers between devices, on_device(): lax.all_to_all(jnp.stack(jnp.split(tokens, lax.axis_size('dp'), axis=1),...  24.9 us
    ppermute x8, starting transfers between devices, shifted(): return lax.ppermute(block, axis, route)  20.3 us
    unnamed x44, local copies, waits for them, and re-layouts  18.7 us
    all_gather x1, waiting for transfers between devices, on_device(): lax.all_gather(dqkv[None], 'dp', axis=0, tiled=True, axis_index_groups=[r...  13.8 us
    ppermute x8, waiting for transfers between devices, shifted(): return lax.ppermute(block, axis, route)  13.7 us
    all_to_all x1, starting transfers between devices, on_device(): lax.all_to_all(jnp.stack(jnp.split(tokens, lax.axis_size('dp'), axis=1),...  7.62 us
  transfers between devices with their start and end apart: 12, of which 6 were waited for; matrix products, arithmetic and copies ran while one was open for 22% of the time, Pallas kernels for 0%

profile of v1, /device:TPU:97, one launch (start us, length us, event | category | flops | bytes accessed | tf_op | source)
XLA Modules:
  0.0 262.5 jit_solution(14459390521832753031)
XLA Ops:
  7.2 2.4 copy.74
  21.4 7.6 %all-to-all-start = ((bf16[16,256,256]{2,1,0:T(8,128)(2,1)}), bf16[16,256,256]{2,1,0:T(8,128)(2,1)}, u32[]{:S(2)}, u32[]{:S(2)}) async-start(bf16[16,256,256]{2,1,0:T(8,128)(2,1)} %bitcast_dynamic-update-slice_fusion), calls=%async_computation | async-start | bytes 4194304 | tf_op jit(solution)/shard_map/all_to_all | solution.py:70
  29.1 2.5 copy.76
  32.5 4.0 %copy.77 = bf16[256,16,256]{2,0,1:T(8,128)(2,1)} copy(bf16[256,16,256]{0,2,1:T(8,128)(2,1)} %bitcast.128) | data formatting | bytes 4194304 | tf_op jit(solution)/shard_map/reshape | solution.py:41
  41.6 6.4 %copy.78 = bf16[256,16,2,256]{0,3,2,1:T(8,128)(2,1)} copy(bf16[256,16,2,256]{3,0,1,2:T(8,128)(2,1)} %pad_maximum_fusion.1) | data formatting | bytes 8388608 | tf_op jit(solution)/shard_map/concatenate | solution.py:79
  48.6 24.9 %all-to-all-done = bf16[16,256,256]{2,1,0:T(8,128)(2,1)} async-done(((bf16[16,256,256]{2,1,0:T(8,128)(2,1)}), bf16[16,256,256]{2,1,0:T(8,128)(2,1)}, u32[]{:S(2)}, u32[]{:S(2)}) %all-to-all-start) | async-done | bytes 2097184 | tf_op jit(solution)/shard_map/all_to_all | solution.py:70
  73.5 2.3 gather_fusion.2
  78.0 2.4 pad_maximum_fusion
  80.4 31.3 %all-gather.3.cloned.1.call-done = bf16[8192,768]{1,0:T(8,128)(2,1)} async-done(((bf16[512,768]{1,0:T(8,128)(2,1)}), bf16[8192,768]{1,0:T(8,128)(2,1)}) %all-gather.3.cloned.1.call-update) | async-done | bytes 12582928 | tf_op jit(solution)/shard_map/all_gather | solution.py:66
  111.6 7.0 %fusion.15 = bf16[256,512]{1,0:T(8,128)(2,1)S(1)} fusion(bf16[256,8192]{0,1:T(8,128)(2,1)} %bitcast.130, bf16[8192,768]{1,0:T(8,128)(2,1)} %all-gather.3.cloned.1.call-done), kind=kOutput, calls=%fused_computation.40 | convolution fusion | flops 2147614720 | bytes 12845056 | tf_op jit(solution)/shard_map/dot_general | solution.py:91
  120.2 3.2 %collective-permute-start.1 = (bf16[256,2,2,128]{3,0,2,1:T(8,128)(2,1)S(1)}, bf16[256,2,2,128]{3,0,2,1:T(8,128)(2,1)S(1)}, u32[]{:S(2)}, u32[]{:S(2)}) collective-permute-start(bf16[256,2,2,128]{3,0,2,1:T(8,128)(2,1)S(1)} %copy.79), channel_id=1, source_target_pairs={{0,48},{16,64},{32,80},{48,96},{64,112},{80,128},{96,144},{112,160... | collective-permute-start | bytes 786440 | tf_op jit(solution)/shard_map/ppermute | solution.py:14
  123.4 4.8 %collective-permute-start.2 = (bf16[256,2,2,128]{3,0,2,1:T(8,128)(2,1)S(1)}, bf16[256,2,2,128]{3,0,2,1:T(8,128)(2,1)S(1)}, u32[]{:S(2)}, u32[]{:S(2)}) collective-permute-start(bf16[256,2,2,128]{3,0,2,1:T(8,128)(2,1)S(1)} %copy.79), channel_id=1, source_target_pairs={{0,32},{16,48},{32,64},{48,80},{64,96},{80,112},{96,128},{112,144}... | collective-permute-start | bytes 786440 | tf_op jit(solution)/shard_map/ppermute | solution.py:14
  128.2 4.9 %collective-permute-start.3 = (bf16[256,2,2,128]{3,0,2,1:T(8,128)(2,1)S(1)}, bf16[256,2,2,128]{3,0,2,1:T(8,128)(2,1)S(1)}, u32[]{:S(2)}, u32[]{:S(2)}) collective-permute-start(bf16[256,2,2,128]{3,0,2,1:T(8,128)(2,1)S(1)} %copy.79), channel_id=1, source_target_pairs={{0,16},{16,32},{32,48},{48,64},{64,80},{80,96},{96,112},{112,128},... | collective-permute-start | bytes 786440 | tf_op jit(solution)/shard_map/ppermute | solution.py:14
  133.1 5.2 %fusion.19 = bf16[256,256]{0,1:T(8,128)(2,1)S(1)} fusion(bf16[256,8192]{0,1:T(8,128)(2,1)} %bitcast.131, bf16[8192,768]{1,0:T(8,128)(2,1)} %all-gather.3.cloned.1.call-done), kind=kOutput, calls=%fused_computation.43 | convolution fusion | flops 1073807360 | bytes 8519680 | tf_op jit(solution)/shard_map/dot_general | solution.py:99
  139.6 2.6 fusion.33
  152.5 2.7 %collective-permute-done.7 = bf16[256,2,2,128]{0,3,2,1:T(8,128)(2,1)S(1)} collective-permute-done((bf16[256,2,2,128]{0,3,2,1:T(8,128)(2,1)S(1)}, bf16[256,2,2,128]{0,3,2,1:T(8,128)(2,1)S(1)}, u32[]{:S(2)}, u32[]{:S(2)}) %collective-permute-start.7) | collective-permute-done | bytes 262176 | tf_op jit(solution)/shard_map/ppermute | solution.py:14
  155.3 10.9 %collective-permute-done.6 = bf16[256,2,2,128]{0,3,2,1:T(8,128)(2,1)S(1)} collective-permute-done((bf16[256,2,2,128]{0,3,2,1:T(8,128)(2,1)S(1)}, bf16[256,2,2,128]{0,3,2,1:T(8,128)(2,1)S(1)}, u32[]{:S(2)}, u32[]{:S(2)}) %collective-permute-start.6) | collective-permute-done | bytes 262176 | tf_op jit(solution)/shard_map/ppermute | solution.py:14
  167.5 4.6 %fusion.3 = f32[256,16,256]{2,0,1:T(8,128)S(1)} fusion(bf16[256,768,1]{0,1,2:T(8,128)(2,1)S(1)} %bitcast.140, bf16[16,2,256,768]{3,2,1,0:T(8,128)(2,1)} %bitcast.133), kind=kOutput, calls=%fused_computation.8 | convolution fusion | flops 1610612736 | bytes 10878976 | tf_op jit(solution)/shard_map/dot_general | solution.py:156
  172.1 4.6 %fusion.13 = bf16[16,256,256]{2,1,0:T(8,128)(2,1)S(1)} fusion(f32[256,16,256]{2,0,1:T(8,128)S(1)} %fusion.3, bf16[256,768,1]{0,1,2:T(8,128)(2,1)S(1)} %bitcast.138, bf16[16,2,256,768]{3,2,1,0:T(8,128)(2,1)} %bitcast.134), kind=kOutput, calls=%fused_computation.31 | convolution fusion | flops 1612709888 | bytes 12976128 | tf_op jit(solution)/shard_map/dot_general | solution.py:151
  178.8 6.9 %all-to-all-start.1 = ((bf16[16,256,256]{2,1,0:T(8,128)(2,1)}), bf16[16,256,256]{2,1,0:T(8,128)(2,1)S(1)}, u32[]{:S(2)}, u32[]{:S(2)}) async-start(bf16[16,256,256]{2,1,0:T(8,128)(2,1)} %gather_fusion.3), calls=%async_computation.1 | async-start | bytes 4194304 | tf_op jit(solution)/shard_map/all_to_all | solution.py:165
  185.7 2.6 convolution_convert_fusion
  189.0 42.2 %all-to-all-done.1 = bf16[16,256,256]{2,1,0:T(8,128)(2,1)S(1)} async-done(((bf16[16,256,256]{2,1,0:T(8,128)(2,1)}), bf16[16,256,256]{2,1,0:T(8,128)(2,1)S(1)}, u32[]{:S(2)}, u32[]{:S(2)}) %all-to-all-start.1) | async-done | bytes 2097184 | tf_op jit(solution)/shard_map/all_to_all | solution.py:165
  232.2 13.8 %all-gather.5.cloned.1.call-done = bf16[16,256,768]{2,1,0:T(8,128)(2,1)} async-done(((bf16[1,256,768]{2,1,0:T(8,128)(2,1)}), bf16[16,256,768]{2,1,0:T(8,128)(2,1)}) %all-gather.5.cloned.1.call-update) | async-done | bytes 6291472 | tf_op jit(solution)/shard_map/all_gather | solution.py:167
  246.0 7.5 %bitcast_convert_fusion = bf16[512,768]{1,0:T(8,128)(2,1)S(1)} fusion(bf16[16,256,512]{2,1,0:T(8,128)(2,1)} %bitcast.129, bf16[16,256,768]{2,1,0:T(8,128)(2,1)} %all-gather.5.cloned.1.call-done), kind=kOutput, calls=%fused_computation.36 | convolution fusion | flops 3221618688 | bytes 11272192 | tf_op jit(solution)/shard_map/dot_general | solution.py:168
  (93 shorter events, 40.5 us)
Async XLA Ops:
  7.2 3.6 %copy-start = (bf16[256,4096]{1,0:T(8,128)(2,1)S(1)}, bf16[256,4096]{1,0:T(8,128)(2,1)}, u32[]{:S(2)}) copy-start(bf16[256,4096]{1,0:T(8,128)(2,1)} %param.11) | copy-start | bytes 6291460
  7.2 104.5 %all-gather.3.cloned.1.call-start = ((), (), s32[]{:S(2)}) async-start(), calls=%async_computation.2 | async-start | bytes 13369344 | tf_op jit(solution)/shard_map/all_gather | solution.py:66
  21.4 52.1 %all-to-all-start = ((bf16[16,256,256]{2,1,0:T(8,128)(2,1)}), bf16[16,256,256]{2,1,0:T(8,128)(2,1)}, u32[]{:S(2)}, u32[]{:S(2)}) async-start(bf16[16,256,256]{2,1,0:T(8,128)(2,1)} %bitcast_dynamic-update-slice_fusion), calls=%async_computation | async-start | bytes 4194304 | tf_op jit(solution)/shard_map/all_to_all | solution.py:70
  29.1 2.6 copy-start.9
  29.1 2.8 %copy-start.8 = (s32[16]{0:T(128)S(1)}, s32[16]{0:T(128)}, u32[]{:S(2)}) copy-start(s32[16]{0:T(128)} %constant.77.clone) | copy-start | bytes 196
  29.1 217.0 %all-gather.5.cloned.1.call-start = ((), (), s32[]{:S(2)}) async-start(), calls=%async_computation.3 | async-start | bytes 6684672 | tf_op jit(solution)/shard_map/all_gather | solution.py:167
  41.6 6.4 %copy-start.6 = (s32[4096]{0:T(1024)S(1)}, s32[4096]{0:T(1024)}, u32[]{:S(2)}) copy-start(s32[4096]{0:T(1024)} %param.14) | copy-start | bytes 49156
  41.6 6.5 %copy-start.5 = (bf16[256,256]{1,0:T(8,128)(2,1)S(1)}, bf16[256,256]{1,0:T(8,128)(2,1)}, u32[]{:S(2)}) copy-start(bf16[256,256]{1,0:T(8,128)(2,1)} %param.15) | copy-start | bytes 393220
  118.8 19.6 %collective-permute-start = (bf16[256,2,2,128]{3,0,2,1:T(8,128)(2,1)S(1)}, bf16[256,2,2,128]{3,0,2,1:T(8,128)(2,1)S(1)}, u32[]{:S(2)}, u32[]{:S(2)}) collective-permute-start(bf16[256,2,2,128]{3,0,2,1:T(8,128)(2,1)S(1)} %copy.79), channel_id=1, source_target_pairs={{0,64},{16,80},{32,96},{48,112},{64,128},{80,144},{96,160},{112,17... | collective-permute-start | bytes 786440 | tf_op jit(solution)/shard_map/ppermute | solution.py:14
  120.2 18.2 %collective-permute-start.1 = (bf16[256,2,2,128]{3,0,2,1:T(8,128)(2,1)S(1)}, bf16[256,2,2,128]{3,0,2,1:T(8,128)(2,1)S(1)}, u32[]{:S(2)}, u32[]{:S(2)}) collective-permute-start(bf16[256,2,2,128]{3,0,2,1:T(8,128)(2,1)S(1)} %copy.79), channel_id=1, source_target_pairs={{0,48},{16,64},{32,80},{48,96},{64,112},{80,128},{96,144},{112,160... | collective-permute-start | bytes 786440 | tf_op jit(solution)/shard_map/ppermute | solution.py:14
  123.4 15.0 %collective-permute-start.2 = (bf16[256,2,2,128]{3,0,2,1:T(8,128)(2,1)S(1)}, bf16[256,2,2,128]{3,0,2,1:T(8,128)(2,1)S(1)}, u32[]{:S(2)}, u32[]{:S(2)}) collective-permute-start(bf16[256,2,2,128]{3,0,2,1:T(8,128)(2,1)S(1)} %copy.79), channel_id=1, source_target_pairs={{0,32},{16,48},{32,64},{48,80},{64,96},{80,112},{96,128},{112,144}... | collective-permute-start | bytes 786440 | tf_op jit(solution)/shard_map/ppermute | solution.py:14
  128.2 10.3 %collective-permute-start.3 = (bf16[256,2,2,128]{3,0,2,1:T(8,128)(2,1)S(1)}, bf16[256,2,2,128]{3,0,2,1:T(8,128)(2,1)S(1)}, u32[]{:S(2)}, u32[]{:S(2)}) collective-permute-start(bf16[256,2,2,128]{3,0,2,1:T(8,128)(2,1)S(1)} %copy.79), channel_id=1, source_target_pairs={{0,16},{16,32},{32,48},{48,64},{64,80},{80,96},{96,112},{112,128},... | collective-permute-start | bytes 786440 | tf_op jit(solution)/shard_map/ppermute | solution.py:14
  138.6 1.0 copy-start.2
  142.2 2.6 %copy-start.1 = (f32[2,256,1280]{2,1,0:T(8,128)}, f32[2,256,1280]{2,1,0:T(8,128)S(1)}, u32[]{:S(2)}) copy-start(f32[2,256,1280]{2,1,0:T(8,128)S(1)} %get-tuple-element.33) | copy-start | bytes 7864324
  145.6 6.3 %copy-start.3 = (bf16[1280,2,2,128]{3,0,2,1:T(8,128)(2,1)S(1)}, bf16[1280,2,2,128]{3,0,2,1:T(8,128)(2,1)}, u32[]{:S(2)}) copy-start(bf16[1280,2,2,128]{3,0,2,1:T(8,128)(2,1)} %copy-done.2) | copy-start | bytes 3932164
  146.0 9.3 %collective-permute-start.7 = (bf16[256,2,2,128]{0,3,2,1:T(8,128)(2,1)S(1)}, bf16[256,2,2,128]{0,3,2,1:T(8,128)(2,1)S(1)}, u32[]{:S(2)}, u32[]{:S(2)}) collective-permute-start(bf16[256,2,2,128]{0,3,2,1:T(8,128)(2,1)S(1)} %get-tuple-element.29), channel_id=1, source_target_pairs={{64,0},{80,16},{96,32},{112,48},{128,64},{144,80},{160,96},{176,11... | collective-permute-start | bytes 786440 | tf_op jit(solution)/shard_map/ppermute | solution.py:14
  147.4 18.8 %collective-permute-start.6 = (bf16[256,2,2,128]{0,3,2,1:T(8,128)(2,1)S(1)}, bf16[256,2,2,128]{0,3,2,1:T(8,128)(2,1)S(1)}, u32[]{:S(2)}, u32[]{:S(2)}) collective-permute-start(bf16[256,2,2,128]{0,3,2,1:T(8,128)(2,1)S(1)} %get-tuple-element.30), channel_id=1, source_target_pairs={{48,0},{64,16},{80,32},{96,48},{112,64},{128,80},{144,96},{160,112... | collective-permute-start | bytes 786440 | tf_op jit(solution)/shard_map/ppermute | solution.py:14
  148.7 17.5 %collective-permute-start.5 = (bf16[256,2,2,128]{0,3,2,1:T(8,128)(2,1)S(1)}, bf16[256,2,2,128]{0,3,2,1:T(8,128)(2,1)S(1)}, u32[]{:S(2)}, u32[]{:S(2)}) collective-permute-start(bf16[256,2,2,128]{0,3,2,1:T(8,128)(2,1)S(1)} %get-tuple-element.31), channel_id=1, source_target_pairs={{32,0},{48,16},{64,32},{80,48},{96,64},{112,80},{128,96},{144,112}... | collective-permute-start | bytes 786440 | tf_op jit(solution)/shard_map/ppermute | solution.py:14
  150.0 16.2 %collective-permute-start.4 = (bf16[256,2,2,128]{0,3,2,1:T(8,128)(2,1)S(1)}, bf16[256,2,2,128]{0,3,2,1:T(8,128)(2,1)S(1)}, u32[]{:S(2)}, u32[]{:S(2)}) collective-permute-start(bf16[256,2,2,128]{0,3,2,1:T(8,128)(2,1)S(1)} %get-tuple-element.28), channel_id=1, source_target_pairs={{16,0},{32,16},{48,32},{64,48},{80,64},{96,80},{112,96},{128,112},... | collective-permute-start | bytes 786440 | tf_op jit(solution)/shard_map/ppermute | solution.py:14
  166.4 1.0 copy-start.7
  178.8 6.9 %copy-start.4 = (bf16[1280,2,2,128]{3,0,2,1:T(8,128)(2,1)S(1)}, bf16[1280,2,2,128]{3,0,2,1:T(8,128)(2,1)}, u32[]{:S(2)}) copy-start(bf16[1280,2,2,128]{3,0,2,1:T(8,128)(2,1)} %copy-done.2) | copy-start | bytes 3932164
  178.8 52.5 %all-to-all-start.1 = ((bf16[16,256,256]{2,1,0:T(8,128)(2,1)}), bf16[16,256,256]{2,1,0:T(8,128)(2,1)S(1)}, u32[]{:S(2)}, u32[]{:S(2)}) async-start(bf16[16,256,256]{2,1,0:T(8,128)(2,1)} %gather_fusion.3), calls=%async_computation.1 | async-start | bytes 4194304 | tf_op jit(solution)/shard_map/all_to_all | solution.py:165
Sparse Core Ops, SparseCore 0:
  10.9 100.6 all-gather.2
  167.5 78.4 all-gather.4
